TPU v7x, 256 devices: a whole 4x4x8 slice. The times are simulated.
256 devices in a mesh: ctx: 32 (over x_lo, z, core), exp: 8 (over y, x_hi).
Axes of the slice: x: 4 (x_hi: 2, x_lo: 2; x = x_hi * 2 + x_lo), y: 4, z: 8, core: 2. Of those that a mesh axis runs over, the one named last changes fastest.
Arguments:
- hidden: bfloat16 [8192, 2048], P(('ctx', 'exp')), may hold values from -1.5 to 1.5
- lengths: int32 [2], replicated, may hold values from 2048 to 4096, as said below
- routes: int32 [8192, 8], P(('ctx', 'exp')), may hold values from 0 to 127, all different within a row; in each aligned block of 32 rows (0 to 31, 32 to 63, ...) at most 4 rows name the same one
- gates: float32 [8192, 8], P(('ctx', 'exp')), may hold values from 0.05 to 0.5
- attn_gain: float32 [2048], replicated, may hold values from 0.25 to 1.75
- q_weight: bfloat16 [2048, 4096], P('ctx', 'exp'), may hold values from -0.125 to 0.125
- key_value_weight: bfloat16 [2048, 1024], P('ctx'), may hold values from -0.125 to 0.125
- q_gain: float32 [128], replicated, may hold values from 0.25 to 1.75
- k_gain: float32 [128], replicated, may hold values from 0.25 to 1.75
- o_weight: bfloat16 [4096, 2048], P('exp', 'ctx'), may hold values from -0.09375 to 0.09375
- moe_gain: float32 [2048], replicated, may hold values from 0.25 to 1.75
- expert_in: bfloat16 [256, 2048, 768], P(('ctx', 'exp')), may hold values from -0.125 to 0.125
- expert_out: bfloat16 [256, 384, 2048], P(('ctx', 'exp')), may hold values from -0.21875 to 0.21875
Outputs:
- new_hidden: bfloat16 [8192, 2048], P(('ctx', 'exp'))
- cache: bfloat16 [2, 8192, 512], P(None, 'ctx', 'exp')
Inputs may be any that keep to these rules, and one draw needn't show every extreme that they name: `lengths`: one of the two prompts has exactly 4096 positions; the other has 2048 to 4096. `routes`: A row names 8 different experts. Within the 32 rows of each device (aligned blocks of rows) no expert is named more than 4 times, a bound that some block reaches.
All inputs are finite; a program needn't handle non-finite values.
Results may differ from a plain program's by a relative error of at most 0.02.
Values may be sent and summed in bfloat16 or wider, within the bound.
No kernel may reach another device: no remote copies, remote signals or barrier semaphores. Data moves between devices by JAX's collectives and lax.ppermute only.
A program may use at most 128 MiB of HBM per device.

v0:
```python
import jax
import jax.numpy as jnp
from jax import lax
from jax.sharding import PartitionSpec as P

MODEL_WIDTH = 2048
QUERY_HEADS = 32
KEY_VALUE_HEADS = 4
HEAD_SIZE = 128
EXPERTS = 128
TOP = 8
epsilon = 1e-06
rope_base = 1000000.0


def from_behind(block, axis, distance):
    devices = range(lax.axis_size(axis))
    route = [((i - distance) % len(devices), i) for i in devices]
    return lax.ppermute(block, axis, route)


def rms_scale(values, gain):
    mean_square = jnp.mean(values * values, axis=-1, keepdims=True)
    return values * lax.rsqrt(mean_square + epsilon) * gain


def mirrored_position(row_ids, count_ctx, tok_ctx):
    half_rows = tok_ctx // 2
    holder = row_ids // tok_ctx
    within = row_ids % tok_ctx
    block_no = jnp.where(within < half_rows, holder, 2 * count_ctx - 1 - holder)
    return block_no * half_rows + within % half_rows


def document_info(token_positions, lengths):
    first_end = lengths[0]
    second_end = lengths[0] + lengths[1]
    document = (token_positions >= first_end).astype(jnp.int32) + (
        token_positions >= second_end
    ).astype(jnp.int32)
    doc_start = jnp.where(document == 0, 0, jnp.where(document == 1, first_end, second_end))
    return (document, token_positions - doc_start)


def rotate(values, rope_pos):
    head_width = values.shape[-1]
    freq_ids = jnp.arange(head_width // 2, dtype=jnp.float32)
    inverse = rope_base ** (-2.0 * freq_ids / head_width)
    angles = rope_pos.astype(jnp.float32)[:, None] * inverse[None, :]
    cosine = jnp.cos(angles)[:, None, :]
    sine_part = jnp.sin(angles)[:, None, :]
    first_half = values[..., : head_width // 2]
    second_half = values[..., head_width // 2 :]
    return jnp.concatenate(
        [
            first_half * cosine - second_half * sine_part,
            second_half * cosine + first_half * sine_part,
        ],
        axis=-1,
    )


def shards(
    hidden,
    lengths,
    routes,
    gates,
    attn_gain,
    q_weight,
    key_value_weight,
    q_gain,
    k_gain,
    o_weight,
    moe_gain,
    expert_in,
    expert_out,
):
    count_ctx = lax.axis_size("ctx")
    expert_count = lax.axis_size("exp")
    my_ctx = lax.axis_index("ctx")
    my_exp = lax.axis_index("exp")
    tok_dev = hidden.shape[0]
    tok_ctx = tok_dev * expert_count
    half_rows = tok_ctx // 2
    head_groups = QUERY_HEADS // KEY_VALUE_HEADS
    q_dev = QUERY_HEADS // expert_count
    key_value_share = max(1, KEY_VALUE_HEADS // expert_count)
    group_dev = q_dev // key_value_share
    column_share = KEY_VALUE_HEADS * HEAD_SIZE // expert_count
    key_value_leading = my_exp * q_dev // head_groups
    col_offset = my_exp * column_share - key_value_leading * HEAD_SIZE
    score_scale = HEAD_SIZE ** (-0.5)
    query_pos = mirrored_position(
        my_ctx * tok_ctx + jnp.arange(tok_ctx, dtype=jnp.int32), count_ctx, tok_ctx
    )
    query_doc, query_rope = document_info(query_pos, lengths)
    normed_own = rms_scale(hidden.astype(jnp.float32), attn_gain).astype(jnp.bfloat16)
    normed = lax.all_gather(normed_own, "exp", axis=0, tiled=True)
    key_cols = lax.dynamic_slice_in_dim(
        key_value_weight, key_value_leading * HEAD_SIZE, key_value_share * HEAD_SIZE, 1
    )
    value_column_block = lax.dynamic_slice_in_dim(
        key_value_weight,
        KEY_VALUE_HEADS * HEAD_SIZE + key_value_leading * HEAD_SIZE,
        key_value_share * HEAD_SIZE,
        1,
    )
    kv_local = jnp.concatenate([key_cols, value_column_block], axis=1)
    q_width = q_dev * HEAD_SIZE
    weights_all = lax.all_gather(
        jnp.concatenate([q_weight, kv_local], axis=1), "ctx", axis=0, tiled=True
    )
    projected = jnp.dot(normed, weights_all, preferred_element_type=jnp.float32)
    q_raw = projected[:, :q_width]
    key_value_plain = projected[:, q_width:]
    queries = rotate(
        rms_scale(q_raw.reshape(tok_ctx, q_dev, HEAD_SIZE), q_gain), query_rope
    ).astype(jnp.bfloat16)
    key_row_block = rotate(
        rms_scale(
            key_value_plain[:, : key_value_share * HEAD_SIZE].reshape(
                tok_ctx, key_value_share, HEAD_SIZE
            ),
            k_gain,
        ),
        query_rope,
    ).astype(jnp.bfloat16)
    value_row_block = key_value_plain[:, key_value_share * HEAD_SIZE :].astype(jnp.bfloat16)
    key_values = jnp.stack(
        [key_row_block.reshape(tok_ctx, key_value_share * HEAD_SIZE), value_row_block]
    )
    query_groups = queries.reshape(tok_ctx, key_value_share, group_dev, HEAD_SIZE)

    def attend(state_now, block_kv, offset):
        length_now = block_kv.shape[1]
        key_pos = mirrored_position(
            offset + jnp.arange(length_now, dtype=jnp.int32), count_ctx, tok_ctx
        )
        key_doc, unused_rope = document_info(key_pos, lengths)
        allowed = (query_doc[:, None] == key_doc[None, :]) & (
            key_pos[None, :] <= query_pos[:, None]
        )
        key_part = block_kv[0].reshape(length_now, key_value_share, HEAD_SIZE)
        value_part = block_kv[1].reshape(length_now, key_value_share, HEAD_SIZE)
        scores = (
            jnp.einsum("qkgd,skd->kgqs", query_groups, key_part, preferred_element_type=jnp.float32)
            * score_scale
        )
        weights = jnp.where(allowed[None, None], jnp.exp(scores), 0.0).astype(jnp.bfloat16)
        numerator = state_now[0] + jnp.einsum(
            "kgqs,skd->qkgd", weights, value_part, preferred_element_type=jnp.float32
        )
        denominator = state_now[1] + jnp.sum(weights, axis=-1, dtype=jnp.float32)
        return (numerator, denominator) + tuple(state_now[2:])

    initial = (
        jnp.zeros((tok_ctx, key_value_share, group_dev, HEAD_SIZE), jnp.float32),
        jnp.zeros((key_value_share, group_dev, tok_ctx), jnp.float32),
    )
    every_kv = lax.all_gather(key_values, "ctx", axis=1, tiled=True)
    total_rows = every_kv.shape[1]
    chunk = min(1024, total_rows)

    def turn(step_no, state_now):
        block_kv = lax.dynamic_slice_in_dim(every_kv, step_no * chunk, chunk, 1)
        return attend(state_now, block_kv, step_no * chunk)

    final_state = lax.fori_loop(0, total_rows // chunk, turn, initial)
    context = (
        (final_state[0] / jnp.transpose(final_state[1], (2, 0, 1))[..., None])
        .astype(jnp.bfloat16)
        .reshape(tok_ctx, q_dev * HEAD_SIZE)
    )

    def block_start(block_no):
        holder = jnp.where(block_no < count_ctx, block_no, 2 * count_ctx - 1 - block_no)
        return holder * tok_ctx + jnp.where(block_no < count_ctx, 0, half_rows)

    first_part = lax.dynamic_slice(
        every_kv, (0, block_start(2 * my_ctx), col_offset), (2, half_rows, column_share)
    )
    second_part = lax.dynamic_slice(
        every_kv, (0, block_start(2 * my_ctx + 1), col_offset), (2, half_rows, column_share)
    )
    cache = jnp.concatenate([first_part, second_part], axis=1)
    attn_part = jnp.dot(
        context,
        lax.all_gather(o_weight, "ctx", axis=1, tiled=True),
        preferred_element_type=jnp.float32,
    )
    attn_own = lax.psum_scatter(
        attn_part.astype(jnp.bfloat16), "exp", scatter_dimension=0, tiled=True
    ).astype(jnp.float32)
    residual_mid = hidden.astype(jnp.float32) + attn_own
    moe_in = rms_scale(residual_mid, moe_gain).astype(jnp.bfloat16)
    devices = count_ctx * expert_count
    slices = max(1, devices // EXPERTS)
    rows_dev = expert_in.shape[0]
    ffs_dev = expert_out.shape[1]
    capacity = max(4, 2 * tok_dev * TOP // EXPERTS)
    route_ids = routes.reshape(-1)
    route_count = route_ids.shape[0]
    expert_hot = (route_ids[:, None] == jnp.arange(EXPERTS, dtype=jnp.int32)[None, :]).astype(
        jnp.int32
    )
    ranking = jnp.sum(jnp.cumsum(expert_hot, axis=0) * expert_hot, axis=1) - 1
    slot_ids = route_ids * capacity + ranking
    slot_hot = (
        slot_ids[:, None] == jnp.arange(EXPERTS * capacity, dtype=jnp.int32)[None, :]
    ).astype(jnp.bfloat16)
    token_hot = (
        (jnp.arange(route_count, dtype=jnp.int32) // TOP)[:, None]
        == jnp.arange(tok_dev, dtype=jnp.int32)[None, :]
    ).astype(jnp.bfloat16)
    placement_map = jnp.einsum(
        "rs,rt->st", slot_hot, token_hot, preferred_element_type=jnp.float32
    ).astype(jnp.bfloat16)
    outgoing = jnp.dot(placement_map, moe_in, preferred_element_type=jnp.float32).astype(
        jnp.bfloat16
    )
    experts_ctx = EXPERTS // count_ctx
    outgoing = outgoing.reshape(count_ctx, experts_ctx * capacity, MODEL_WIDTH)
    landed = lax.all_to_all(outgoing, "ctx", split_axis=0, concat_axis=0, tiled=True)
    landed = jnp.broadcast_to(
        landed.reshape(count_ctx, experts_ctx, 1, capacity, MODEL_WIDTH),
        (count_ctx, experts_ctx, slices, capacity, MODEL_WIDTH),
    ).reshape(count_ctx, expert_count, capacity, MODEL_WIDTH)
    arrived = lax.all_to_all(landed, "exp", split_axis=1, concat_axis=1, tiled=True)
    arrived = arrived.reshape(count_ctx, expert_count, rows_dev, capacity, MODEL_WIDTH)
    gate_up = jnp.einsum("abrcd,rdf->abrcf", arrived, expert_in, preferred_element_type=jnp.float32)
    activated = (jax.nn.silu(gate_up[..., :ffs_dev]) * gate_up[..., ffs_dev:]).astype(jnp.bfloat16)
    produced = jnp.einsum(
        "abrcf,rfd->abrcd", activated, expert_out, preferred_element_type=jnp.float32
    ).astype(jnp.bfloat16)
    produced = produced.reshape(count_ctx, expert_count, rows_dev * capacity, MODEL_WIDTH)
    came_back = lax.all_to_all(produced, "exp", split_axis=1, concat_axis=1, tiled=True)
    part_sum = jnp.sum(
        came_back.reshape(count_ctx, experts_ctx, slices, capacity, MODEL_WIDTH),
        axis=2,
        dtype=jnp.float32,
    ).astype(jnp.bfloat16)
    returned = lax.all_to_all(
        part_sum.reshape(count_ctx, experts_ctx * capacity, MODEL_WIDTH),
        "ctx",
        split_axis=0,
        concat_axis=0,
        tiled=True,
    )
    slice_sum = returned.reshape(EXPERTS * capacity, MODEL_WIDTH).astype(jnp.float32)
    gate_hot = slot_hot.astype(jnp.float32) * gates.reshape(-1)[:, None]
    combiner = jnp.einsum(
        "rs,rt->ts", gate_hot, token_hot.astype(jnp.float32), precision=lax.Precision.HIGHEST
    )
    moe_out = jnp.dot(combiner, slice_sum, precision=lax.Precision.HIGHEST)
    new_hidden = (residual_mid + moe_out).astype(jnp.bfloat16)
    return (new_hidden, cache)


def solution(mesh):
    in_specs = (
        P(("ctx", "exp"), None),
        P(),
        P(("ctx", "exp"), None),
        P(("ctx", "exp"), None),
        P(),
        P("ctx", "exp"),
        P("ctx", None),
        P(),
        P(),
        P("exp", "ctx"),
        P(),
        P(("ctx", "exp"), None, None),
        P(("ctx", "exp"), None, None),
    )
    out_specs = (P(("ctx", "exp"), None), P(None, "ctx", "exp"))
    return jax.shard_map(shards, mesh=mesh, in_specs=in_specs, out_specs=out_specs, check_vma=False)
```

profile of v0, /device:TPU:32, one launch (start us, length us, event | category | flops | bytes accessed | tf_op | source)
XLA Modules:
  0.0 614.3 jit_solution(10730122127005586213)
XLA Ops:
  15.8 49.4 %all-gather.5.cloned.1.call-done = bf16[256,2048]{1,0:T(8,128)(2,1)} async-done(((bf16[32,2048]{1,0:T(8,128)(2,1)}), bf16[256,2048]{1,0:T(8,128)(2,1)}) %all-gather.5.cloned.1.call-update) | async-done | bytes 1048592 | tf_op jit(solution)/shard_map/all_gather | solution.py:98
  65.2 65.6 %all-gather.7.cloned.1.call-done = bf16[2048,768]{1,0:T(8,128)(2,1)} async-done(((bf16[64,768]{1,0:T(8,128)(2,1)}), bf16[2048,768]{1,0:T(8,128)(2,1)}) %all-gather.7.cloned.1.call-update) | async-done | bytes 3145744 | tf_op jit(solution)/shard_map/all_gather | solution.py:110
  130.8 3.2 fusion.85
  136.9 2.3 fusion.83
  144.3 57.5 %all-gather.9.cloned.1.call-done = bf16[2,8192,128]{2,1,0:T(8,128)(2,1)} async-done(((bf16[2,256,128]{2,1,0:T(8,128)(2,1)}), bf16[2,8192,128]{2,1,0:T(8,128)(2,1)}) %all-gather.9.cloned.1.call-update) | async-done | bytes 4194320 | tf_op jit(solution)/shard_map/all_gather | solution.py:160
  201.9 44.5 %while.21 = (s32[]{:T(128)}, f32[256,1,4,128]{0,3,2,1:T(8,128)}, f32[1,4,256]{2,1,0:T(4,128)S(1)}, bf16[2,8192,128]{2,1,0:T(8,128)(2,1)}, s32[2]{0:T(128)S(1)}, ...) while((s32[]{:T(128)}, f32[256,1,4,128]{0,3,2,1:T(8,128)}, ...), condition=%wide.region_5.6_spmd.clone.clone.clone, body=%wide.region_3.5_spmd.clone.clone.clone.sunk | while | flops 543215872 | bytes 10785070 | solution.py:168
  247.5 20.4 %all-gather.11.cloned.1.call-done = bf16[512,2048]{0,1:T(8,128)(2,1)} async-done(((bf16[512,64]{0,1:T(8,128)(2,1)}), bf16[512,2048]{0,1:T(8,128)(2,1)}) %all-gather.11.cloned.1.call-update) | async-done | bytes 2097168 | tf_op jit(solution)/shard_map/all_gather | solution.py:188
  267.9 3.3 convolution_convert_fusion.2
  272.1 77.6 %reduce-scatter.2.cloned.1.call-done = bf16[32,2048]{1,0:T(8,128)(2,1)} async-done(((bf16[256,2048]{1,0:T(8,128)(2,1)}), bf16[32,2048]{1,0:T(8,128)(2,1)}) %reduce-scatter.2.cloned.1.call-update) | async-done | bytes 131088 | tf_op jit(solution)/shard_map/reduce_scatter | solution.py:191
  350.8 3.2 convolution_convert_fusion.1
  354.0 59.3 %all_to_all.20 = bf16[32,16,2048]{2,1,0:T(8,128)(2,1)} all-to-all(bf16[32,16,2048]{2,1,0:T(8,128)(2,1)} %bitcast.128), channel_id=1, replica_groups=mesh['ctx'=32,'exp'=8] {'ctx'}, dimensions={0} | all-to-all | bytes 4194304 | tf_op jit(solution)/shard_map/all_to_all | solution.py:223
  413.4 4.2 broadcast_in_dim.90
  417.5 2.6 copy.100
  420.1 2.6 broadcast_in_dim.91
  422.7 54.6 %all_to_all.21 = bf16[32,8,4,2048]{3,2,0,1:T(4,128)(2,1)S(1)} all-to-all(bf16[32,8,4,2048]{3,2,0,1:T(4,128)(2,1)S(1)} %bitcast.127), channel_id=1, replica_groups=mesh['ctx'=32,'exp'=8] {'exp'}, dimensions={1} | all-to-all | bytes 8388608 | tf_op jit(solution)/shard_map/all_to_all | solution.py:228
  477.3 5.0 fusion.32
  482.3 2.4 convolution_convert_fusion
  484.7 3.2 copy.102
  487.9 51.5 %all_to_all.22 = bf16[32,8,4,2048]{3,2,0,1:T(4,128)(2,1)S(1)} all-to-all(bf16[32,8,4,2048]{3,2,0,1:T(4,128)(2,1)S(1)} %copy.102), channel_id=1, replica_groups=mesh['ctx'=32,'exp'=8] {'exp'}, dimensions={1} | all-to-all | bytes 8388608 | tf_op jit(solution)/shard_map/all_to_all | solution.py:236
  539.4 3.4 bitcast_reduce_fusion
  543.9 2.5 copy.105
  546.4 6.4 %all-to-all-start.3 = ((bf16[32,16,2048]{2,1,0:T(8,128)(2,1)}), bf16[32,16,2048]{2,1,0:T(8,128)(2,1)}, u32[]{:S(2)}, u32[]{:S(2)}) async-start(bf16[32,16,2048]{2,1,0:T(8,128)(2,1)} %copy.105), calls=%async_computation.4 | async-start | bytes 4194304 | tf_op jit(solution)/shard_map/all_to_all | solution.py:242
  555.9 48.5 %all-to-all-done.3 = bf16[32,16,2048]{2,1,0:T(8,128)(2,1)} async-done(((bf16[32,16,2048]{2,1,0:T(8,128)(2,1)}), bf16[32,16,2048]{2,1,0:T(8,128)(2,1)}, u32[]{:S(2)}, u32[]{:S(2)}) %all-to-all-start.3) | async-done | bytes 2097184 | tf_op jit(solution)/shard_map/all_to_all | solution.py:242
  604.4 3.4 fusion.31
  (159 shorter events, 66.4 us)
Async XLA Ops:
  7.2 470.2 %copy-start = (bf16[1,2048,768]{2,1,0:T(8,128)(2,1)S(1)}, bf16[1,2048,768]{2,1,0:T(8,128)(2,1)}, u32[]{:S(2)}) copy-start(bf16[1,2048,768]{2,1,0:T(8,128)(2,1)} %param.26) | copy-start | bytes 9437188
  7.2 58.0 %all-gather.5.cloned.1.call-start = ((), (), s32[]{:S(2)}) async-start(), calls=%async_computation.5 | async-start | bytes 1179648 | tf_op jit(solution)/shard_map/all_gather | solution.py:98
  10.1 120.7 %all-gather.7.cloned.1.call-start = ((), (), s32[]{:S(2)}) async-start(), calls=%async_computation.6 | async-start | bytes 3244032 | tf_op jit(solution)/shard_map/all_gather | solution.py:110
  10.2 124.0 %copy-start.10 = (f32[128]{0:T(128)S(1)}, f32[128]{0:T(128)}, u32[]{:S(2)}) copy-start(f32[128]{0:T(128)} %param.23) | copy-start | bytes 1540
  12.5 189.4 %all-gather.9.cloned.1.call-start = ((), (), s32[]{:S(2)}) async-start(), calls=%async_computation.7 | async-start | bytes 4325376 | tf_op jit(solution)/shard_map/all_gather | solution.py:160
  134.0 8.6 %copy-start.11 = (f32[128]{0:T(128)S(1)}, f32[128]{0:T(128)}, u32[]{:S(2)}) copy-start(f32[128]{0:T(128)} %param.22) | copy-start | bytes 1540
  135.7 132.2 %all-gather.11.cloned.1.call-start = ((), (), s32[]{:S(2)}) async-start(), calls=%async_computation.8 | async-start | bytes 2162688 | tf_op jit(solution)/shard_map/all_gather | solution.py:188
  136.3 213.5 %reduce-scatter.2.cloned.1.call-start = ((), (), s32[]{:S(2)}) async-start(), calls=%async_computation.9 | async-start | bytes 1179648 | tf_op jit(solution)/shard_map/reduce_scatter | solution.py:191
  139.1 62.7 %copy-start.6 = (s32[2]{0:T(128)S(1)}, s32[2]{0:T(128)}, u32[]{:S(2)}) copy-start(s32[2]{0:T(128)} %param.16) | copy-start | bytes 28
  202.9 2.2 copy-start.1
  208.5 2.2 copy-start.1
  214.0 2.2 copy-start.1
  219.6 2.2 copy-start.1
  225.2 2.2 copy-start.1
  230.7 2.2 copy-start.1
  236.3 2.2 copy-start.1
  241.8 2.2 copy-start.1
  246.3 24.9 %copy-start.8 = (s32[32,8]{0,1:T(8,128)S(1)}, s32[32,8]{0,1:T(8,128)}, u32[]{:S(2)}) copy-start(s32[32,8]{0,1:T(8,128)} %param.17) | copy-start | bytes 3076
  246.3 103.4 %copy-start.3 = (bf16[32,2048]{1,0:T(8,128)(2,1)S(1)}, bf16[32,2048]{1,0:T(8,128)(2,1)}, u32[]{:S(2)}) copy-start(bf16[32,2048]{1,0:T(8,128)(2,1)} %param.15) | copy-start | bytes 393220
  246.3 104.5 %copy-start.7 = (f32[2048]{0:T(1024)S(1)}, f32[2048]{0:T(1024)}, u32[]{:S(2)}) copy-start(f32[2048]{0:T(1024)} %param.25) | copy-start | bytes 24580
  477.3 5.0 copy-start.12
  546.4 6.5 %copy-start.9 = (f32[32,8]{0,1:T(8,128)S(1)}, f32[32,8]{0,1:T(8,128)}, u32[]{:S(2)}) copy-start(f32[32,8]{0,1:T(8,128)} %param.18) | copy-start | bytes 3076
  546.4 57.9 %copy-start.4 = (bf16[32,2048]{1,0:T(8,128)(2,1)S(1)}, bf16[32,2048]{1,0:T(8,128)(2,1)}, u32[]{:S(2)}) copy-start(bf16[32,2048]{1,0:T(8,128)(2,1)} %reduce-scatter.2.cloned.1.call-done) | copy-start | bytes 393220
  546.4 57.9 %all-to-all-start.3 = ((bf16[32,16,2048]{2,1,0:T(8,128)(2,1)}), bf16[32,16,2048]{2,1,0:T(8,128)(2,1)}, u32[]{:S(2)}, u32[]{:S(2)}) async-start(bf16[32,16,2048]{2,1,0:T(8,128)(2,1)} %copy.105), calls=%async_computation.4 | async-start | bytes 4194304 | tf_op jit(solution)/shard_map/all_to_all | solution.py:242
  (9 other events, 7.3 us)
Sparse Core Ops, SparseCore 0:
  11.2 53.9 all-gather.4
  67.1 63.6 all-gather.6
  135.8 66.0 all-gather.8
  203.6 64.2 all-gather.10
  271.6 78.0 reduce-scatter.1
where the time goes:
time: 616 us; the launch traced here: 614 us
  waiting for transfers between devices  320 us (52%)
  blocking collectives  165 us (27%)
  matrix products  50.8 us (8%)
  local copies, waits for them, and re-layouts  31.3 us (5%)
  other arithmetic  24.7 us (4%)
  between operations  15.4 us (2%)
  starting transfers between devices  6.63 us (1%)
    reduce_scatter x1, waiting for transfers between devices, shards(): lax.psum_scatter(attn_part.astype(jnp.bfloat16), 'exp', scatter_dimension...  77.6 us
    all_gather x1, waiting for transfers between devices, shards(): lax.all_gather(jnp.concatenate([q_weight, kv_local], axis=1), 'ctx', axis...  65.6 us
    all_to_all x1, blocking collectives, shards(): lax.all_to_all(outgoing, 'ctx', split_axis=0, concat_axis=0, tiled=True)  59.3 us
    all_gather x1, waiting for transfers between devices, shards(): every_kv = lax.all_gather(key_values, 'ctx', axis=1, tiled=True)  57.5 us
    all_to_all x1, blocking collectives, shards(): lax.all_to_all(landed, 'exp', split_axis=1, concat_axis=1, tiled=True)  54.6 us
    all_to_all x1, blocking collectives, shards(): lax.all_to_all(produced, 'exp', split_axis=1, concat_axis=1, tiled=True)  51.5 us
    all_gather x1, waiting for transfers between devices, shards(): normed = lax.all_gather(normed_own, 'exp', axis=0, tiled=True)  49.4 us
    all_to_all x1, waiting for transfers between devices, shards(): lax.all_to_all(part_sum.reshape(count_ctx, experts_ctx * capacity, MODEL_...  48.5 us
  transfers between devices with their start and end apart: 6, of which 6 were waited for; matrix products, arithmetic and copies ran while one was open for 9% of the time, Pallas kernels for 0%

commit v1 on v0

--- a/solution.py
+++ b/solution.py
@@ -157,7 +157,9 @@
         jnp.zeros((tok_ctx, key_value_share, group_dev, HEAD_SIZE), jnp.float32),
         jnp.zeros((key_value_share, group_dev, tok_ctx), jnp.float32),
     )
-    every_kv = lax.all_gather(key_values, "ctx", axis=1, tiled=True)
+    every_kv = jnp.concatenate(
+        lax.all_to_all(jnp.stack([key_values] * lax.axis_size("ctx")), "ctx", 0, 0), axis=1
+    )
     total_rows = every_kv.shape[1]
     chunk = min(1024, total_rows)
 

time: 616 us -> 648 us (1.052)
  waiting for transfers between devices: 320 us -> 336 us
  local copies, waits for them, and re-layouts: 31.3 us -> 40 us
  starting transfers between devices: 6.63 us -> 14.2 us
    all_to_all x0 -> x1, waiting for transfers between devices: none -> 97.7 us  [shards(): lax.all_to_all(jnp.stack([key_values] * lax.axis_size('ctx')), 'ctx', 0, 0)]
    all_gather x1 -> x0, waiting for transfers between devices: 57.5 us -> none  [shards(): every_kv = lax.all_gather(key_values, 'ctx', axis=1, tiled=True)]
    all_gather x1, waiting for transfers between devices: 20.4 us -> 0.02 us  [shards(): lax.all_gather(o_weight, 'ctx', axis=1, tiled=True)]
    all_to_all x0 -> x1, starting transfers between devices: none -> 7.57 us  [shards(): lax.all_to_all(jnp.stack([key_values] * lax.axis_size('ctx')), 'ctx', 0, 0)]
  transfers between devices with their start and end apart: 6 -> 6, of which waited for: 6 -> 5; matrix products, arithmetic and copies ran while one was open for 9% -> 9% of each run, Pallas kernels for 0% -> 0%
where the time goes in v1:
time: 648 us; the launch traced here: 647 us
  waiting for transfers between devices  336 us (52%)
  blocking collectives  165 us (25%)
  matrix products  50.8 us (8%)
  local copies, waits for them, and re-layouts  40 us (6%)
  other arithmetic  24.3 us (4%)
  between operations  15.5 us (2%)
  starting transfers between devices  14.2 us (2%)
    all_to_all x1, waiting for transfers between devices, shards(): lax.all_to_all(jnp.stack([key_values] * lax.axis_size('ctx')), 'ctx', 0, 0)  97.7 us
    reduce_scatter x1, waiting for transfers between devices, shards(): lax.psum_scatter(attn_part.astype(jnp.bfloat16), 'exp', scatter_dimension...  74.3 us
    all_gather x1, waiting for transfers between devices, shards(): lax.all_gather(jnp.concatenate([q_weight, kv_local], axis=1), 'ctx', axis...  65.6 us
    all_to_all x1, blocking collectives, shards(): lax.all_to_all(outgoing, 'ctx', split_axis=0, concat_axis=0, tiled=True)  59.3 us
    all_to_all x1, blocking collectives, shards(): lax.all_to_all(landed, 'exp', split_axis=1, concat_axis=1, tiled=True)  54.5 us
    all_to_all x1, blocking collectives, shards(): lax.all_to_all(produced, 'exp', split_axis=1, concat_axis=1, tiled=True)  51.5 us
    all_gather x1, waiting for transfers between devices, shards(): normed = lax.all_gather(normed_own, 'exp', axis=0, tiled=True)  49.4 us
    all_to_all x1, waiting for transfers between devices, shards(): lax.all_to_all(part_sum.reshape(count_ctx, experts_ctx * capacity, MODEL_...  48.5 us
  transfers between devices with their start and end apart: 6, of which 5 were waited for; matrix products, arithmetic and copies ran while one was open for 9% of the time, Pallas kernels for 0%

profile of v1, /device:TPU:32, one launch (start us, length us, event | category | flops | bytes accessed | tf_op | source)
XLA Modules:
  0.0 646.8 jit_solution(16787845431506172240)
XLA Ops:
  15.8 49.4 %all-gather.4.cloned.1.call-done = bf16[256,2048]{1,0:T(8,128)(2,1)} async-done(((bf16[32,2048]{1,0:T(8,128)(2,1)}), bf16[256,2048]{1,0:T(8,128)(2,1)}) %all-gather.4.cloned.1.call-update) | async-done | bytes 1048592 | tf_op jit(solution)/shard_map/all_gather | solution.py:98
  65.2 65.6 %all-gather.6.cloned.1.call-done = bf16[2048,768]{1,0:T(8,128)(2,1)} async-done(((bf16[64,768]{1,0:T(8,128)(2,1)}), bf16[2048,768]{1,0:T(8,128)(2,1)}) %all-gather.6.cloned.1.call-update) | async-done | bytes 3145744 | tf_op jit(solution)/shard_map/all_gather | solution.py:110
  130.8 3.2 fusion.85
  135.1 2.5 stack.8
  137.6 7.6 %all-to-all-start = ((bf16[32,2,256,128]{2,3,1,0:T(8,128)(2,1)}), bf16[32,2,256,128]{2,3,1,0:T(8,128)(2,1)}, u32[]{:S(2)}, u32[]{:S(2)}) async-start(bf16[32,2,256,128]{2,3,1,0:T(8,128)(2,1)} %stack.8), calls=%async_computation | async-start | bytes 8388608 | tf_op jit(solution)/shard_map/all_to_all | solution.py:161
  153.9 97.7 %all-to-all-done = bf16[32,2,256,128]{2,3,1,0:T(8,128)(2,1)} async-done(((bf16[32,2,256,128]{2,3,1,0:T(8,128)(2,1)}), bf16[32,2,256,128]{2,3,1,0:T(8,128)(2,1)}, u32[]{:S(2)}, u32[]{:S(2)}) %all-to-all-start) | async-done | bytes 4194336 | tf_op jit(solution)/shard_map/all_to_all | solution.py:161
  251.6 6.4 copy.103
  257.9 44.6 %while.21 = (s32[]{:T(128)}, f32[256,1,4,128]{0,3,2,1:T(8,128)}, f32[1,4,256]{2,1,0:T(4,128)S(1)}, bf16[2,8192,128]{2,1,0:T(8,128)(2,1)}, s32[2]{0:T(128)S(1)}, ...) while((s32[]{:T(128)}, f32[256,1,4,128]{0,3,2,1:T(8,128)}, ...), condition=%wide.region_5.6_spmd.clone.clone.clone, body=%wide.region_3.5_spmd.clone.clone.clone.sunk | while | flops 543215872 | bytes 10785070 | solution.py:170
  303.7 3.3 convolution_convert_fusion.2
  307.9 74.3 %reduce-scatter.2.cloned.1.call-done = bf16[32,2048]{1,0:T(8,128)(2,1)} async-done(((bf16[256,2048]{1,0:T(8,128)(2,1)}), bf16[32,2048]{1,0:T(8,128)(2,1)}) %reduce-scatter.2.cloned.1.call-update) | async-done | bytes 131088 | tf_op jit(solution)/shard_map/reduce_scatter | solution.py:193
  383.3 3.2 convolution_convert_fusion.1
  386.5 59.3 %all_to_all.25 = bf16[32,16,2048]{2,1,0:T(8,128)(2,1)} all-to-all(bf16[32,16,2048]{2,1,0:T(8,128)(2,1)} %bitcast.131), channel_id=1, replica_groups=mesh['ctx'=32,'exp'=8] {'ctx'}, dimensions={0} | all-to-all | bytes 4194304 | tf_op jit(solution)/shard_map/all_to_all | solution.py:225
  445.9 4.2 broadcast_in_dim.90
  450.0 2.6 copy.111
  452.6 2.6 broadcast_in_dim.91
  455.2 54.5 %all_to_all.26 = bf16[32,8,4,2048]{3,2,0,1:T(4,128)(2,1)S(1)} all-to-all(bf16[32,8,4,2048]{3,2,0,1:T(4,128)(2,1)S(1)} %bitcast.130), channel_id=1, replica_groups=mesh['ctx'=32,'exp'=8] {'exp'}, dimensions={1} | all-to-all | bytes 8388608 | tf_op jit(solution)/shard_map/all_to_all | solution.py:230
  509.8 5.0 fusion.32
  517.1 3.2 copy.113
  520.4 51.5 %all_to_all.27 = bf16[32,8,4,2048]{3,2,0,1:T(4,128)(2,1)S(1)} all-to-all(bf16[32,8,4,2048]{3,2,0,1:T(4,128)(2,1)S(1)} %copy.113), channel_id=1, replica_groups=mesh['ctx'=32,'exp'=8] {'exp'}, dimensions={1} | all-to-all | bytes 8388608 | tf_op jit(solution)/shard_map/all_to_all | solution.py:238
  571.9 3.4 bitcast_reduce_fusion
  576.4 2.5 copy.116
  578.9 6.4 all-to-all-start.4
  588.3 48.5 %all-to-all-done.4 = bf16[32,16,2048]{2,1,0:T(8,128)(2,1)} async-done(((bf16[32,16,2048]{2,1,0:T(8,128)(2,1)}), bf16[32,16,2048]{2,1,0:T(8,128)(2,1)}, u32[]{:S(2)}, u32[]{:S(2)}) %all-to-all-start.4) | async-done | bytes 2097184 | tf_op jit(solution)/shard_map/all_to_all | solution.py:244
  636.8 3.4 fusion.31
  (163 shorter events, 70.7 us)
Async XLA Ops:
  7.2 502.6 %copy-start = (bf16[1,2048,768]{2,1,0:T(8,128)(2,1)S(1)}, bf16[1,2048,768]{2,1,0:T(8,128)(2,1)}, u32[]{:S(2)}) copy-start(bf16[1,2048,768]{2,1,0:T(8,128)(2,1)} %param.26) | copy-start | bytes 9437188
  7.2 58.0 %all-gather.4.cloned.1.call-start = ((), (), s32[]{:S(2)}) async-start(), calls=%async_computation.6 | async-start | bytes 1179648 | tf_op jit(solution)/shard_map/all_gather | solution.py:98
  10.1 120.7 %all-gather.6.cloned.1.call-start = ((), (), s32[]{:S(2)}) async-start(), calls=%async_computation.7 | async-start | bytes 3244032 | tf_op jit(solution)/shard_map/all_gather | solution.py:110
  10.2 124.0 %copy-start.11 = (f32[128]{0:T(128)S(1)}, f32[128]{0:T(128)}, u32[]{:S(2)}) copy-start(f32[128]{0:T(128)} %param.23) | copy-start | bytes 1540
  137.6 114.0 %all-to-all-start = ((bf16[32,2,256,128]{2,3,1,0:T(8,128)(2,1)}), bf16[32,2,256,128]{2,3,1,0:T(8,128)(2,1)}, u32[]{:S(2)}, u32[]{:S(2)}) async-start(bf16[32,2,256,128]{2,3,1,0:T(8,128)(2,1)} %stack.8), calls=%async_computation | async-start | bytes 8388608 | tf_op jit(solution)/shard_map/all_to_all | solution.py:161
  145.1 7.0 %copy-start.12 = (f32[128]{0:T(128)S(1)}, f32[128]{0:T(128)}, u32[]{:S(2)}) copy-start(f32[128]{0:T(128)} %param.22) | copy-start | bytes 1540
  145.2 158.5 %all-gather.8.cloned.1.call-start = ((), (), s32[]{:S(2)}) async-start(), calls=%async_computation.8 | async-start | bytes 2162688 | tf_op jit(solution)/shard_map/all_gather | solution.py:190
  145.9 236.3 %reduce-scatter.2.cloned.1.call-start = ((), (), s32[]{:S(2)}) async-start(), calls=%async_computation.9 | async-start | bytes 1179648 | tf_op jit(solution)/shard_map/reduce_scatter | solution.py:193
  153.9 104.1 %copy-start.7 = (s32[2]{0:T(128)S(1)}, s32[2]{0:T(128)}, u32[]{:S(2)}) copy-start(s32[2]{0:T(128)} %param.16) | copy-start | bytes 28
  259.0 2.2 copy-start.2
  264.6 2.2 copy-start.2
  270.2 2.2 copy-start.2
  275.8 2.1 copy-start.2
  281.3 2.2 copy-start.2
  286.9 2.2 copy-start.2
  298.1 2.2 copy-start.2
  302.6 4.5 copy-start.9
  302.6 79.7 %copy-start.4 = (bf16[32,2048]{1,0:T(8,128)(2,1)S(1)}, bf16[32,2048]{1,0:T(8,128)(2,1)}, u32[]{:S(2)}) copy-start(bf16[32,2048]{1,0:T(8,128)(2,1)} %param.15) | copy-start | bytes 393220
  302.6 80.7 %copy-start.8 = (f32[2048]{0:T(1024)S(1)}, f32[2048]{0:T(1024)}, u32[]{:S(2)}) copy-start(f32[2048]{0:T(1024)} %param.25) | copy-start | bytes 24580
  509.8 5.0 copy-start.13
  576.4 63.8 %copy-start.1 = (bf16[1,2048,768]{2,1,0:T(8,128)(2,1)S(1)}, bf16[1,2048,768]{2,1,0:T(8,128)(2,1)}, u32[]{:S(2)}) copy-start(bf16[1,2048,768]{2,1,0:T(8,128)(2,1)} %param.26) | copy-start | bytes 9437188
  578.9 6.5 %copy-start.10 = (f32[32,8]{0,1:T(8,128)S(1)}, f32[32,8]{0,1:T(8,128)}, u32[]{:S(2)}) copy-start(f32[32,8]{0,1:T(8,128)} %param.18) | copy-start | bytes 3076
  578.9 57.9 %copy-start.5 = (bf16[32,2048]{1,0:T(8,128)(2,1)S(1)}, bf16[32,2048]{1,0:T(8,128)(2,1)}, u32[]{:S(2)}) copy-start(bf16[32,2048]{1,0:T(8,128)(2,1)} %reduce-scatter.2.cloned.1.call-done) | copy-start | bytes 393220
  578.9 57.9 %all-to-all-start.4 = ((bf16[32,16,2048]{2,1,0:T(8,128)(2,1)}), bf16[32,16,2048]{2,1,0:T(8,128)(2,1)}, u32[]{:S(2)}, u32[]{:S(2)}) async-start(bf16[32,16,2048]{2,1,0:T(8,128)(2,1)} %copy.116), calls=%async_computation.5 | async-start | bytes 4194304 | tf_op jit(solution)/shard_map/all_to_all | solution.py:244
  (10 other events, 9.4 us)
Sparse Core Ops, SparseCore 0:
  11.2 53.9 all-gather.3
  67.1 63.6 all-gather.5
  147.8 80.3 all-gather.7
  307.2 74.9 reduce-scatter.1
